TPU v7x, 256 devices: a whole 4x4x8 slice. The times are simulated.
256 devices in a mesh: ctx: 64 (over z, y_hi, x), tp: 4 (over y_lo, core).
Axes of the slice: x: 4, y: 4 (y_hi: 2, y_lo: 2; y = y_hi * 2 + y_lo), z: 8, core: 2. Of those that a mesh axis runs over, the one named last changes fastest.
Arguments:
- query_in: bfloat16 [2048, 8192], P('tp', 'ctx'), may hold values from -6 to 6
- key_in: bfloat16 [2048, 8192], P('tp', 'ctx'), may hold values from -6 to 6
- value_in: bfloat16 [2048, 8192], P('tp', 'ctx'), may hold values from -6 to 6
- short_weights: float32 [3, 2048, 7], P(None, 'tp'), may hold values from -3 to 3
- filters: float32 [4, 512, 8192], P('tp', 'ctx'), may hold values from 0 to 1
- out_weight: bfloat16 [4096, 2048], P(None, 'tp'), may hold values from -0.125 to 0.125
- cotangent: bfloat16 [4096, 8192], P('tp', 'ctx'), may hold values from -16 to 16
Outputs:
- mixed_out: bfloat16 [4096, 8192], P('tp', 'ctx')
- grad_query: bfloat16 [2048, 8192], P('tp', 'ctx')
- grad_key: bfloat16 [2048, 8192], P('tp', 'ctx')
- grad_value: bfloat16 [2048, 8192], P('tp', 'ctx')
- grad_filters: float32 [4, 512, 8192], P('tp', 'ctx')
- grad_out_weight: float32 [4096, 2048], P('ctx', 'tp')
All inputs are finite; a program needn't handle non-finite values.
Results may differ from a plain program's by a relative error of at most 0.012.
Values may be sent and summed in bfloat16 or wider, within the bound.
No kernel may reach another device: no remote copies, remote signals or barrier semaphores. Data moves between devices by JAX's collectives and lax.ppermute only.
A program may use at most 128 MiB of HBM per device.

v0:
```python
import math
import jax
import jax.numpy as jnp
from jax import lax
from jax.sharding import PartitionSpec as P

BLOCK = 128
TWO_PI = 2.0 * math.pi
HIGHEST = lax.Precision.HIGHEST


def from_behind(value, axis, steps):
    count = lax.axis_size(axis)
    first, last = (max(0, -steps), min(count, count - steps))
    return lax.ppermute(value, axis, [(source, source + steps) for source in range(first, last)])


def fourier_table(count):
    element_indices = jnp.arange(count, dtype=jnp.int32)
    angles = (element_indices[:, None] * element_indices[None, :] % count).astype(jnp.float32) * (
        TWO_PI / count
    )
    return (jnp.cos(angles), -jnp.sin(angles))


def make_tables(length, block_width):
    row_count = 2 * length // block_width
    full_len = row_count * block_width
    outer_re, outer_im = fourier_table(row_count)
    inner_re, inner_im = fourier_table(block_width)
    row_index = jnp.arange(row_count, dtype=jnp.int32)[:, None]
    col_index = jnp.arange(block_width, dtype=jnp.int32)[None, :]
    angles = (row_index * col_index % full_len).astype(jnp.float32) * (TWO_PI / full_len)
    return (outer_re, outer_im, inner_re, inner_im, jnp.cos(angles), -jnp.sin(angles))


def spectrum(signal, tables):
    outer_re, outer_im, inner_re, inner_im, twist_re, twist_im = tables
    channels, length = signal.shape
    block_width = inner_re.shape[0]
    half_rows = length // block_width
    blocks = signal.reshape(channels, half_rows, block_width)
    section_re = jnp.einsum("kn,cnm->ckm", outer_re[:, :half_rows], blocks, precision=HIGHEST)
    section_im = jnp.einsum("kn,cnm->ckm", outer_im[:, :half_rows], blocks, precision=HIGHEST)
    turned_re = section_re * twist_re - section_im * twist_im
    turned_im = section_re * twist_im + section_im * twist_re
    frequency_real_component = jnp.matmul(turned_re, inner_re, precision=HIGHEST) - jnp.matmul(
        turned_im, inner_im, precision=HIGHEST
    )
    spec_im = jnp.matmul(turned_re, inner_im, precision=HIGHEST) + jnp.matmul(
        turned_im, inner_re, precision=HIGHEST
    )
    return (frequency_real_component, spec_im)


def inverse(frequency_real_component, spec_im, tables):
    outer_re, outer_im, inner_re, inner_im, twist_re, twist_im = tables
    channels, row_count, block_width = frequency_real_component.shape
    half_rows = row_count // 2
    back_re = jnp.matmul(frequency_real_component, inner_re, precision=HIGHEST) + jnp.matmul(
        spec_im, inner_im, precision=HIGHEST
    )
    back_im = jnp.matmul(spec_im, inner_re, precision=HIGHEST) - jnp.matmul(
        frequency_real_component, inner_im, precision=HIGHEST
    )
    turned_re = back_re * twist_re + back_im * twist_im
    turned_im = back_im * twist_re - back_re * twist_im
    signal = jnp.einsum("nk,ckm->cnm", outer_re[:half_rows], turned_re, precision=HIGHEST)
    signal = signal + jnp.einsum("nk,ckm->cnm", outer_im[:half_rows], turned_im, precision=HIGHEST)
    return (signal / (row_count * block_width)).reshape(channels, half_rows * block_width)


def causal_taps(stacked, earlier, weights):
    tap_count = weights.shape[2]
    length = stacked.shape[2]
    extended = jnp.concatenate([earlier, stacked], axis=2).astype(jnp.float32)
    running_total = jnp.zeros(stacked.shape, jnp.float32)
    for offset in range(tap_count):
        begin = tap_count - 1 - offset
        running_total = (
            running_total
            + weights[:, :, offset : offset + 1] * extended[:, :, begin : begin + length]
        )
    return running_total


def anticausal_taps(stacked, following, weights):
    tap_count = weights.shape[2]
    length = stacked.shape[2]
    extended = jnp.concatenate([stacked, following], axis=2).astype(jnp.float32)
    running_total = jnp.zeros(stacked.shape, jnp.float32)
    for offset in range(tap_count):
        running_total = (
            running_total
            + weights[:, :, offset : offset + 1] * extended[:, :, offset : offset + length]
        )
    return running_total


def to_channels(block):
    return lax.all_to_all(block, "ctx", split_axis=0, concat_axis=1, tiled=True)


def to_positions(block):
    return lax.all_to_all(block, "ctx", split_axis=1, concat_axis=0, tiled=True)


def per_device(query_in, key_in, value_in, short_weights, filters, out_weight, cotangent):
    tap_count = short_weights.shape[2]
    local_len = query_in.shape[1]
    stacked = jnp.stack([query_in, key_in, value_in])
    earlier = from_behind(stacked[:, :, local_len - (tap_count - 1) :], "ctx", 1)
    shorts = causal_taps(stacked, earlier, short_weights).astype(jnp.bfloat16)
    product = (shorts[1].astype(jnp.float32) * shorts[2].astype(jnp.float32)).astype(jnp.bfloat16)
    product_chan = to_channels(product)
    tables = make_tables(product_chan.shape[1], BLOCK)
    kernel_re, kernel_im = spectrum(filters[0], tables)
    product_re, product_im = spectrum(product_chan.astype(jnp.float32), tables)
    convolved_chan = inverse(
        product_re * kernel_re - product_im * kernel_im,
        product_re * kernel_im + product_im * kernel_re,
        tables,
    ).astype(jnp.bfloat16)
    convolved = to_positions(convolved_chan)
    gated_out = (shorts[0].astype(jnp.float32) * convolved.astype(jnp.float32)).astype(jnp.bfloat16)
    mixed_out = lax.psum_scatter(
        jnp.dot(out_weight, gated_out, preferred_element_type=jnp.float32).astype(jnp.bfloat16),
        "tp",
        scatter_dimension=0,
        tiled=True,
    )
    full_cotangent = lax.all_gather(cotangent, "tp", axis=0, tiled=True)
    grad_gated = lax.dot_general(
        out_weight, full_cotangent, (((0,), (0,)), ((), ())), preferred_element_type=jnp.float32
    )
    grad_out_weight = lax.psum_scatter(
        lax.dot_general(
            full_cotangent, gated_out, (((1,), (1,)), ((), ())), preferred_element_type=jnp.float32
        ),
        "ctx",
        scatter_dimension=0,
        tiled=True,
    )
    grad_conv = (grad_gated * shorts[0].astype(jnp.float32)).astype(jnp.bfloat16)
    grad_chan = to_channels(grad_conv)
    gradient_re, gradient_im = spectrum(grad_chan.astype(jnp.float32), tables)
    grad_product_chan = inverse(
        kernel_re * gradient_re + kernel_im * gradient_im,
        kernel_re * gradient_im - kernel_im * gradient_re,
        tables,
    ).astype(jnp.bfloat16)
    grad_filters = inverse(
        product_re * gradient_re + product_im * gradient_im,
        product_re * gradient_im - product_im * gradient_re,
        tables,
    ).reshape(filters.shape)
    derivative_of_multiple = to_positions(grad_product_chan)
    grad_shorts = jnp.stack(
        [
            grad_gated * convolved.astype(jnp.float32),
            derivative_of_multiple.astype(jnp.float32) * shorts[2].astype(jnp.float32),
            derivative_of_multiple.astype(jnp.float32) * shorts[1].astype(jnp.float32),
        ]
    ).astype(jnp.bfloat16)
    following = from_behind(grad_shorts[:, :, : tap_count - 1], "ctx", -1)
    gradients = anticausal_taps(grad_shorts, following, short_weights).astype(jnp.bfloat16)
    return (mixed_out, gradients[0], gradients[1], gradients[2], grad_filters, grad_out_weight)


def solution(mesh):
    placed = (
        P("tp", "ctx"),
        P("tp", "ctx"),
        P("tp", "ctx"),
        P(None, "tp", None),
        P("tp", "ctx", None),
        P(None, "tp"),
        P("tp", "ctx"),
    )
    return jax.shard_map(
        per_device,
        mesh=mesh,
        in_specs=placed,
        out_specs=(
            P("tp", "ctx"),
            P("tp", "ctx"),
            P("tp", "ctx"),
            P("tp", "ctx"),
            P("tp", "ctx", None),
            P("ctx", "tp"),
        ),
        check_vma=False,
    )
```

profile of v0, /device:TPU:0, one launch (start us, length us, event | category | flops | bytes accessed | tf_op | source)
XLA Modules:
  0.0 518.8 jit_solution(1460974614563037735)
XLA Ops:
  11.0 1.7 collective-permute-start
  16.7 1.6 convolution_add_fusion.4
  20.5 14.5 %all-to-all-start = ((bf16[64,8,128]{2,1,0:T(8,128)(2,1)}), bf16[64,8,128]{2,1,0:T(8,128)(2,1)}, u32[]{:S(2)}, u32[]{:S(2)}) async-start(bf16[64,8,128]{2,1,0:T(8,128)(2,1)} %bitcast.4), calls=%async_computation | async-start | bytes 262144 | tf_op jit(solution)/shard_map/all_to_all | solution.py:101
  35.0 1.6 convolution_subtract_fusion.4
  36.7 10.6 %all-to-all-done = bf16[64,8,128]{2,1,0:T(8,128)(2,1)} async-done(((bf16[64,8,128]{2,1,0:T(8,128)(2,1)}), bf16[64,8,128]{2,1,0:T(8,128)(2,1)}, u32[]{:S(2)}, u32[]{:S(2)}) %all-to-all-start) | async-done | bytes 131104 | tf_op jit(solution)/shard_map/all_to_all | solution.py:101
  47.3 1.3 convolution_bitcast_fusion.3
  48.6 1.3 convolution_bitcast_fusion.4
  51.2 2.0 convolution_subtract_fusion.5
  53.2 4.0 fusion.54
  57.9 4.6 all-to-all-start.2
  63.1 2.0 fusion.80
  65.1 9.9 %all-to-all-done.2 = bf16[64,8,128]{2,1,0:T(8,128)(2,1)S(1)} async-done(((bf16[64,8,128]{2,1,0:T(8,128)(2,1)}), bf16[64,8,128]{2,1,0:T(8,128)(2,1)S(1)}, u32[]{:S(2)}, u32[]{:S(2)}) %all-to-all-start.2) | async-done | bytes 131104 | tf_op jit(solution)/shard_map/all_to_all | solution.py:101
  79.6 1.2 convolution_subtract_fusion.2
  80.8 1.4 multiply_add_fusion
  87.6 16.5 %all_to_all.49 = bf16[8,64,128]{2,0,1:T(8,128)(2,1)S(1)} all-to-all(bf16[8,64,128]{2,0,1:T(8,128)(2,1)S(1)} %copy.193), channel_id=1, replica_groups=mesh['ctx'=64,'tp'=4] {'ctx'}, dimensions={1} | all-to-all | bytes 262144 | tf_op jit(solution)/shard_map/all_to_all | solution.py:105
  104.3 4.7 fusion
  109.1 5.8 %convolution_bitcast_fusion = f32[4096,512]{0,1:T(8,128)} fusion(bf16[4096,128]{1,0:T(8,128)(2,1)} %all-gather.2.cloned.1.call-done, f32[512,128]{0,1:T(8,128)S(1)} %copy.194, bf16[3,512,128]{1,2,0:T(8,128)(2,1)S(1)} %copy-done.4), kind=kOutput, calls=%fused_computation | convolution fusion | flops 537067520 | bytes 9830400 | tf_op jit(solution)/shard_map/dot_general | solution.py:137
  114.9 9.1 %copy.324 = f32[4096,512]{1,0:T(8,128)} copy(f32[4096,512]{0,1:T(8,128)} %convolution_bitcast_fusion) | data formatting | bytes 16777216
  129.8 4.8 all-to-all-start.3
  139.1 8.1 %all-to-all-done.3 = bf16[8,64,128]{2,0,1:T(8,128)(2,1)S(1)} async-done(((bf16[8,64,128]{2,0,1:T(8,128)(2,1)}), bf16[8,64,128]{2,0,1:T(8,128)(2,1)S(1)}, u32[]{:S(2)}, u32[]{:S(2)}) %all-to-all-start.3) | async-done | bytes 131104 | tf_op jit(solution)/shard_map/all_to_all | solution.py:105
  148.4 1.3 collective-permute-start.1
  151.2 3.0 collective-permute-done.1
  157.3 1.8 copy.233
  159.1 352.9 %reduce-scatter.7.cloned.1.call-done = f32[64,512]{1,0:T(8,128)} async-done(((f32[4096,512]{1,0:T(8,128)}), f32[64,512]{1,0:T(8,128)}) %reduce-scatter.7.cloned.1.call-update) | async-done | bytes 131088
  (120 shorter events, 38.2 us)
Async XLA Ops:
  7.2 6.6 %copy-start = (f32[1,8,8192]{2,1,0:T(8,128)S(1)}, f32[1,8,8192]{2,1,0:T(8,128)}, u32[]{:S(2)}) copy-start(f32[1,8,8192]{2,1,0:T(8,128)} %param.11) | copy-start | bytes 786436
  7.2 9.5 %copy-start.23 = (f32[3,512,7]{1,2,0:T(8,128)S(1)}, f32[3,512,7]{1,2,0:T(8,128)}, u32[]{:S(2)}) copy-start(f32[3,512,7]{1,2,0:T(8,128)} %param.10) | copy-start | bytes 129028
  7.2 46.0 %all-gather.2.cloned.1.call-start = ((), (), s32[]{:S(2)}) async-start(), calls=%async_computation.7 | async-start | bytes 1310720 | tf_op jit(solution)/shard_map/all_gather | solution.py:132
  11.0 7.4 %collective-permute-start = (bf16[3,512,6]{1,2,0:T(8,128)(2,1)S(1)}, bf16[3,512,6]{1,2,0:T(8,128)(2,1)S(1)}, u32[]{:S(2)}, u32[]{:S(2)}) collective-permute-start(bf16[3,512,6]{1,2,0:T(8,128)(2,1)S(1)} %pad_maximum_fusion.2), channel_id=1, source_target_pairs={{0,4},{4,8},{8,12},{12,16},{16,20},{20,24},{24,28},{28,32},{32,36}... | collective-permute-start | bytes 55304 | tf_op jit(solution)/shard_map/ppermute | solution.py:15
  12.9 62.5 %copy-start.11 = (f32[128,128]{0,1:T(8,128)}, f32[128,128]{0,1:T(8,128)S(1)}, u32[]{:S(2)}) copy-start(f32[128,128]{0,1:T(8,128)S(1)} %fusion.126) | copy-start | bytes 196612
  13.2 61.8 %copy-start.9 = (f32[128,128]{0,1:T(8,128)}, f32[128,128]{0,1:T(8,128)S(1)}, u32[]{:S(2)}) copy-start(f32[128,128]{0,1:T(8,128)S(1)} %sine_negate_fusion.1) | copy-start | bytes 196612
  19.7 33.5 %copy-start.3 = (bf16[3,512,128]{1,2,0:T(8,128)(2,1)}, bf16[3,512,128]{1,2,0:T(8,128)(2,1)S(1)}, u32[]{:S(2)}) copy-start(bf16[3,512,128]{1,2,0:T(8,128)(2,1)S(1)} %fusion.17) | copy-start | bytes 1179652
  20.5 26.8 %all-to-all-start = ((bf16[64,8,128]{2,1,0:T(8,128)(2,1)}), bf16[64,8,128]{2,1,0:T(8,128)(2,1)}, u32[]{:S(2)}, u32[]{:S(2)}) async-start(bf16[64,8,128]{2,1,0:T(8,128)(2,1)} %bitcast.4), calls=%async_computation | async-start | bytes 262144 | tf_op jit(solution)/shard_map/all_to_all | solution.py:101
  57.9 17.0 %all-to-all-start.2 = ((bf16[64,8,128]{2,1,0:T(8,128)(2,1)}), bf16[64,8,128]{2,1,0:T(8,128)(2,1)S(1)}, u32[]{:S(2)}, u32[]{:S(2)}) async-start(bf16[64,8,128]{2,1,0:T(8,128)(2,1)} %bitcast.34), calls=%async_computation.3 | async-start | bytes 262144 | tf_op jit(solution)/shard_map/all_to_all | solution.py:101
  62.6 94.8 %reduce-scatter.5.cloned.1.call-start = ((), (), s32[]{:S(2)}) async-start(), calls=%async_computation.6 | async-start | bytes 1310720 | tf_op jit(solution)/shard_map/reduce_scatter | solution.py:126
  75.4 5.4 %copy-start.5 = (f32[8,128,128]{2,1,0:T(8,128)S(1)}, f32[8,128,128]{2,1,0:T(8,128)}, u32[]{:S(2)}) copy-start(f32[8,128,128]{2,1,0:T(8,128)} %convolution_add_fusion.4) | copy-start | bytes 1572868
  75.4 5.4 %copy-start.6 = (f32[8,128,128]{2,1,0:T(8,128)S(1)}, f32[8,128,128]{2,1,0:T(8,128)}, u32[]{:S(2)}) copy-start(f32[8,128,128]{2,1,0:T(8,128)} %convolution_subtract_fusion.4) | copy-start | bytes 1572868
  75.5 5.4 %copy-start.7 = (f32[8,128,128]{2,1,0:T(8,128)S(1)}, f32[8,128,128]{2,1,0:T(8,128)}, u32[]{:S(2)}) copy-start(f32[8,128,128]{2,1,0:T(8,128)} %convolution_subtract_fusion.5) | copy-start | bytes 1572868
  83.1 21.1 %copy-start.4 = (bf16[3,512,128]{1,2,0:T(8,128)(2,1)S(1)}, bf16[3,512,128]{1,2,0:T(8,128)(2,1)}, u32[]{:S(2)}) copy-start(bf16[3,512,128]{1,2,0:T(8,128)(2,1)} %copy-done.3) | copy-start | bytes 1179652
  104.2 10.6 %copy-start.1 = (f32[512,128]{0,1:T(8,128)}, f32[512,128]{0,1:T(8,128)S(1)}, u32[]{:S(2)}) copy-start(f32[512,128]{0,1:T(8,128)S(1)} %copy.194) | copy-start | bytes 786436
  109.0 403.0 %reduce-scatter.7.cloned.1.call-start = ((), (), s32[]{:S(2)}) async-start(), calls=%async_computation.8 | async-start | bytes 8519680
  129.8 17.3 %all-to-all-start.3 = ((bf16[8,64,128]{2,0,1:T(8,128)(2,1)}), bf16[8,64,128]{2,0,1:T(8,128)(2,1)S(1)}, u32[]{:S(2)}, u32[]{:S(2)}) async-start(bf16[8,64,128]{2,0,1:T(8,128)(2,1)} %copy.218), calls=%async_computation.4 | async-start | bytes 262144 | tf_op jit(solution)/shard_map/all_to_all | solution.py:105
  134.7 12.7 %copy-start.2 = (f32[512,128]{0,1:T(8,128)S(1)}, f32[512,128]{0,1:T(8,128)}, u32[]{:S(2)}) copy-start(f32[512,128]{0,1:T(8,128)} %copy-done.1) | copy-start | bytes 786436
  138.3 16.0 %copy-start.14 = (f32[3,512]{1,0:T(4,128)S(1)}, f32[3,512]{1,0:T(4,128)}, u32[]{:S(2)}) copy-start(f32[3,512]{1,0:T(4,128)} %copy-done.13) | copy-start | bytes 18436
  138.3 16.0 %copy-start.16 = (f32[3,512]{1,0:T(4,128)S(1)}, f32[3,512]{1,0:T(4,128)}, u32[]{:S(2)}) copy-start(f32[3,512]{1,0:T(4,128)} %copy-done.15) | copy-start | bytes 18436
  138.3 16.0 %copy-start.18 = (f32[3,512]{1,0:T(4,128)S(1)}, f32[3,512]{1,0:T(4,128)}, u32[]{:S(2)}) copy-start(f32[3,512]{1,0:T(4,128)} %copy-done.17) | copy-start | bytes 18436
  138.3 16.0 %copy-start.20 = (f32[3,512]{1,0:T(4,128)S(1)}, f32[3,512]{1,0:T(4,128)}, u32[]{:S(2)}) copy-start(f32[3,512]{1,0:T(4,128)} %copy-done.19) | copy-start | bytes 18436
  138.3 16.0 %copy-start.22 = (f32[3,512,1]{1,0,2:T(4,128)S(1)}, f32[3,512,1]{1,0,2:T(4,128)}, u32[]{:S(2)}) copy-start(f32[3,512,1]{1,0,2:T(4,128)} %copy-done.21) | copy-start | bytes 18436
  148.4 5.9 %collective-permute-start.1 = (bf16[3,512,6]{1,2,0:T(8,128)(2,1)S(1)}, bf16[3,512,6]{1,2,0:T(8,128)(2,1)S(1)}, u32[]{:S(2)}, u32[]{:S(2)}) collective-permute-start(bf16[3,512,6]{1,2,0:T(8,128)(2,1)S(1)} %pad_maximum_fusion), channel_id=1, source_target_pairs={{4,0},{8,4},{12,8},{16,12},{20,16},{24,20},{28,24},{32,28},{36,32}... | collective-permute-start | bytes 55304 | tf_op jit(solution)/shard_map/ppermute | solution.py:15
  (8 other events, 16.4 us)
Sparse Core Ops, SparseCore 0:
  9.8 24.0 all-gather.1
  109.1 15.6 reduce-scatter.4
  127.9 384.0 reduce-scatter.6
where the time goes:
time: 528 us; the launch traced here: 519 us
  waiting for transfers between devices  385 us (73%)
  matrix products  51 us (10%)
  starting transfers between devices  27.6 us (5%)
  local copies, waits for them, and re-layouts  20.4 us (4%)
  blocking collectives  16.5 us (3%)
  between operations  14.7 us (3%)
    unnamed x4, waiting for transfers between devices  354 us
    all_to_all x2, waiting for transfers between devices, to_channels(): return lax.all_to_all(block, 'ctx', split_axis=0, concat_axis=1, tiled=True)  20.5 us
    all_to_all x2, starting transfers between devices, to_channels(): return lax.all_to_all(block, 'ctx', split_axis=0, concat_axis=1, tiled=True)  19.2 us
    unnamed x60, local copies, waits for them, and re-layouts  16.8 us
    all_to_all x1, blocking collectives, to_positions(): return lax.all_to_all(block, 'ctx', split_axis=1, concat_axis=0, tiled=True)  16.5 us
  transfers between devices with their start and end apart: 8, of which 5 were waited for; matrix products, arithmetic and copies ran while one was open for 10% of the time, Pallas kernels for 0%

commit v1 on v0

--- a/solution.py
+++ b/solution.py
@@ -3,6 +3,7 @@
 import jax.numpy as jnp
 from jax import lax
 from jax.sharding import PartitionSpec as P
+from jax.lax import all_to_all, axis_size
 
 BLOCK = 128
 TWO_PI = 2.0 * math.pi
@@ -98,7 +99,19 @@
 
 
 def to_channels(block):
-    return lax.all_to_all(block, "ctx", split_axis=0, concat_axis=1, tiled=True)
+
+    def lift_terms(d_out, d0, state):
+        return jnp.concatenate(
+            all_to_all(
+                jnp.stack(jnp.split(state, axis_size("ctx"), axis=d_out)),
+                split_axis=0,
+                concat_axis=0,
+                axis_name="ctx",
+            ),
+            axis=d0,
+        )
+
+    return lift_terms(0, 1, block)
 
 
 def to_positions(block):

time: 528 us -> 602 us (1.14)
  local copies, waits for them, and re-layouts: 20.4 us -> 89.2 us
    unnamed x60 -> x190, local copies, waits for them, and re-layouts: 16.8 us -> 85.5 us
    ppermute x2, waiting for transfers between devices: 3.04 us -> 11.5 us  [from_behind(): lax.ppermute(value, axis, [(source, source + steps) for source in range(f...]
    unnamed x4, waiting for transfers between devices: 354 us -> 346 us
  transfers between devices with their start and end apart: 8 -> 8, of which waited for: 5 -> 6; matrix products, arithmetic and copies ran while one was open for 10% -> 15% of each run, Pallas kernels for 0% -> 0%
where the time goes in v1:
time: 602 us; the launch traced here: 595 us
  waiting for transfers between devices  387 us (64%)
  local copies, waits for them, and re-layouts  89.2 us (15%)
  matrix products  47.1 us (8%)
  starting transfers between devices  30.9 us (5%)
  blocking collectives  16.5 us (3%)
  between operations  14.8 us (2%)
  other arithmetic  9.43 us (2%)
    unnamed x4, waiting for transfers between devices  346 us
    unnamed x190, local copies, waits for them, and re-layouts  85.5 us
    all_to_all x2, starting transfers between devices, lift_terms(): all_to_all(jnp.stack(jnp.split(state, axis_size('ctx'), axis=d_out)), spl...  21.9 us
    all_to_all x2, waiting for transfers between devices, lift_terms(): all_to_all(jnp.stack(jnp.split(state, axis_size('ctx'), axis=d_out)), spl...  21 us
    all_to_all x1, blocking collectives, to_positions(): return lax.all_to_all(block, 'ctx', split_axis=1, concat_axis=0, tiled=True)  16.5 us
  transfers between devices with their start and end apart: 8, of which 6 were waited for; matrix products, arithmetic and copies ran while one was open for 15% of the time, Pallas kernels for 0%

profile of v1, /device:TPU:0, one launch (start us, length us, event | category | flops | bytes accessed | tf_op | source)
XLA Modules:
  0.0 594.6 jit_solution(15430812176391054087)
XLA Ops:
  9.1 1.7 collective-permute-start
  14.9 1.6 convolution_add_fusion.4
  16.6 2.5 collective-permute-done
  19.5 3.0 fusion.17
  59.6 17.3 %all-to-all-start = ((bf16[64,8,128]{2,1,0:T(8,128)(2,1)}), bf16[64,8,128]{2,1,0:T(8,128)(2,1)S(1)}, u32[]{:S(2)}, u32[]{:S(2)}) async-start(bf16[64,8,128]{2,1,0:T(8,128)(2,1)} %constant_dynamic-update-slice_fusion), calls=%async_computation | async-start | bytes 262144 | tf_op jit(solution)/shard_map/all_to_all | solution.py:105
  76.9 1.6 convolution_subtract_fusion.4
  78.6 10.8 %all-to-all-done = bf16[64,8,128]{2,1,0:T(8,128)(2,1)S(1)} async-done(((bf16[64,8,128]{2,1,0:T(8,128)(2,1)}), bf16[64,8,128]{2,1,0:T(8,128)(2,1)S(1)}, u32[]{:S(2)}, u32[]{:S(2)}) %all-to-all-start) | async-done | bytes 131104 | tf_op jit(solution)/shard_map/all_to_all | solution.py:105
  91.5 2.0 convolution_subtract_fusion.5
  93.5 4.5 fusion.54
  135.0 4.6 all-to-all-start.2
  139.9 2.0 fusion.79
  141.9 10.2 %all-to-all-done.2 = bf16[64,8,128]{2,1,0:T(8,128)(2,1)S(1)} async-done(((bf16[64,8,128]{2,1,0:T(8,128)(2,1)}), bf16[64,8,128]{2,1,0:T(8,128)(2,1)S(1)}, u32[]{:S(2)}, u32[]{:S(2)}) %all-to-all-start.2) | async-done | bytes 131104 | tf_op jit(solution)/shard_map/all_to_all | solution.py:105
  158.1 2.2 multiply_add_fusion
  165.7 16.5 %all_to_all.30 = bf16[8,64,128]{2,0,1:T(8,128)(2,1)S(1)} all-to-all(bf16[8,64,128]{2,0,1:T(8,128)(2,1)S(1)} %copy.266), channel_id=1, replica_groups=mesh['ctx'=64,'tp'=4] {'ctx'}, dimensions={1} | all-to-all | bytes 262144 | tf_op jit(solution)/shard_map/all_to_all | solution.py:118
  182.2 2.5 fusion
  185.9 4.5 convolution_bitcast_fusion
  190.4 9.1 %copy.390 = f32[4096,512]{1,0:T(8,128)} copy(f32[4096,512]{0,1:T(8,128)} %convolution_bitcast_fusion) | data formatting | bytes 16777216
  205.6 5.7 all-to-all-start.3
  215.7 7.8 %all-to-all-done.3 = bf16[8,64,128]{2,0,1:T(8,128)(2,1)} async-done(((bf16[8,64,128]{2,0,1:T(8,128)(2,1)}), bf16[8,64,128]{2,0,1:T(8,128)(2,1)}, u32[]{:S(2)}, u32[]{:S(2)}) %all-to-all-start.3) | async-done | bytes 131104 | tf_op jit(solution)/shard_map/all_to_all | solution.py:118
  224.6 1.3 collective-permute-start.1
  227.5 8.9 %collective-permute-done.1 = bf16[3,512,6]{2,1,0:T(8,128)(2,1)S(1)} collective-permute-done((bf16[3,512,6]{2,1,0:T(8,128)(2,1)S(1)}, bf16[3,512,6]{2,1,0:T(8,128)(2,1)S(1)}, u32[]{:S(2)}, u32[]{:S(2)}) %collective-permute-start.1) | collective-permute-done | bytes 18464 | tf_op jit(solution)/shard_map/ppermute | solution.py:16
  236.6 3.0 fusion.10
  240.3 1.8 copy.302
  242.1 345.7 %reduce-scatter.7.cloned.1.call-done = f32[64,512]{1,0:T(8,128)} async-done(((f32[4096,512]{1,0:T(8,128)}), f32[64,512]{1,0:T(8,128)}) %reduce-scatter.7.cloned.1.call-update) | async-done | bytes 131088
  (246 shorter events, 109.0 us)
Async XLA Ops:
  7.2 4.7 copy-start
  7.2 86.3 %all-gather.2.cloned.1.call-start = ((), (), s32[]{:S(2)}) async-start(), calls=%async_computation.7 | async-start | bytes 1310720 | tf_op jit(solution)/shard_map/all_gather | solution.py:145
  9.1 10.1 %collective-permute-start = (bf16[3,512,6]{2,1,0:T(8,128)(2,1)S(1)}, bf16[3,512,6]{2,1,0:T(8,128)(2,1)S(1)}, u32[]{:S(2)}, u32[]{:S(2)}) collective-permute-start(bf16[3,512,6]{2,1,0:T(8,128)(2,1)S(1)} %pad_maximum_fusion.2), channel_id=1, source_target_pairs={{0,4},{4,8},{8,12},{12,16},{16,20},{20,24},{24,28},{28,32},{32,36}... | collective-permute-start | bytes 55304 | tf_op jit(solution)/shard_map/ppermute | solution.py:16
  11.1 152.8 %copy-start.11 = (f32[128,128]{0,1:T(8,128)}, f32[128,128]{0,1:T(8,128)S(1)}, u32[]{:S(2)}) copy-start(f32[128,128]{0,1:T(8,128)S(1)} %fusion.127) | copy-start | bytes 196612
  11.4 153.5 %copy-start.8 = (f32[128,128]{0,1:T(8,128)}, f32[128,128]{0,1:T(8,128)S(1)}, u32[]{:S(2)}) copy-start(f32[128,128]{0,1:T(8,128)S(1)} %sine_negate_fusion.1) | copy-start | bytes 196612
  16.6 5.9 copy-start.18
  16.6 5.9 copy-start.20
  16.6 5.9 copy-start.22
  16.6 5.9 copy-start.24
  16.6 5.9 copy-start.26
  59.6 29.7 %all-to-all-start = ((bf16[64,8,128]{2,1,0:T(8,128)(2,1)}), bf16[64,8,128]{2,1,0:T(8,128)(2,1)S(1)}, u32[]{:S(2)}, u32[]{:S(2)}) async-start(bf16[64,8,128]{2,1,0:T(8,128)(2,1)} %constant_dynamic-update-slice_fusion), calls=%async_computation | async-start | bytes 262144 | tf_op jit(solution)/shard_map/all_to_all | solution.py:105
  135.0 17.0 %all-to-all-start.2 = ((bf16[64,8,128]{2,1,0:T(8,128)(2,1)}), bf16[64,8,128]{2,1,0:T(8,128)(2,1)S(1)}, u32[]{:S(2)}, u32[]{:S(2)}) async-start(bf16[64,8,128]{2,1,0:T(8,128)(2,1)} %constant_dynamic-update-slice_fusion.64), calls=%async_computation.3 | async-start | bytes 262144 | tf_op jit(solution)/shard_map/all_to_all | solution.py:105
  139.6 100.7 %reduce-scatter.5.cloned.1.call-start = ((), (), s32[]{:S(2)}) async-start(), calls=%async_computation.6 | async-start | bytes 1310720 | tf_op jit(solution)/shard_map/reduce_scatter | solution.py:139
  163.0 19.2 %copy-start.1 = (bf16[4096,512]{1,0:T(8,128)(2,1)S(1)}, bf16[4096,512]{1,0:T(8,128)(2,1)}, u32[]{:S(2)}) copy-start(bf16[4096,512]{1,0:T(8,128)(2,1)} %param.12) | copy-start | bytes 12582916
  184.7 403.1 %reduce-scatter.7.cloned.1.call-start = ((), (), s32[]{:S(2)}) async-start(), calls=%async_computation.8 | async-start | bytes 8519680
  205.6 17.9 %all-to-all-start.3 = ((bf16[8,64,128]{2,0,1:T(8,128)(2,1)}), bf16[8,64,128]{2,0,1:T(8,128)(2,1)}, u32[]{:S(2)}, u32[]{:S(2)}) async-start(bf16[8,64,128]{2,0,1:T(8,128)(2,1)} %copy.289), calls=%async_computation.4 | async-start | bytes 262144 | tf_op jit(solution)/shard_map/all_to_all | solution.py:118
  214.0 10.5 %copy-start.14 = (f32[512,128]{1,0:T(8,128)S(1)}, f32[512,128]{1,0:T(8,128)}, u32[]{:S(2)}) copy-start(f32[512,128]{1,0:T(8,128)} %get-tuple-element.53) | copy-start | bytes 786436
  214.9 11.0 %copy-start.10 = (f32[128,128]{0,1:T(8,128)S(1)}, f32[128,128]{0,1:T(8,128)}, u32[]{:S(2)}) copy-start(f32[128,128]{0,1:T(8,128)} %copy-done.8) | copy-start | bytes 196612
  224.6 11.8 %collective-permute-start.1 = (bf16[3,512,6]{2,1,0:T(8,128)(2,1)S(1)}, bf16[3,512,6]{2,1,0:T(8,128)(2,1)S(1)}, u32[]{:S(2)}, u32[]{:S(2)}) collective-permute-start(bf16[3,512,6]{2,1,0:T(8,128)(2,1)S(1)} %pad_maximum_fusion), channel_id=1, source_target_pairs={{4,0},{8,4},{12,8},{16,12},{20,16},{24,20},{28,24},{32,28},{36,32}... | collective-permute-start | bytes 55304 | tf_op jit(solution)/shard_map/ppermute | solution.py:16
  226.7 9.9 %copy-start.19 = (f32[3,512]{1,0:T(4,128)S(1)}, f32[3,512]{1,0:T(4,128)}, u32[]{:S(2)}) copy-start(f32[3,512]{1,0:T(4,128)} %copy-done.18) | copy-start | bytes 18436
  226.7 9.9 %copy-start.21 = (f32[3,512]{1,0:T(4,128)S(1)}, f32[3,512]{1,0:T(4,128)}, u32[]{:S(2)}) copy-start(f32[3,512]{1,0:T(4,128)} %copy-done.20) | copy-start | bytes 18436
  226.7 9.9 %copy-start.23 = (f32[3,512]{1,0:T(4,128)S(1)}, f32[3,512]{1,0:T(4,128)}, u32[]{:S(2)}) copy-start(f32[3,512]{1,0:T(4,128)} %copy-done.22) | copy-start | bytes 18436
  226.7 9.9 %copy-start.25 = (f32[3,512]{1,0:T(4,128)S(1)}, f32[3,512]{1,0:T(4,128)}, u32[]{:S(2)}) copy-start(f32[3,512]{1,0:T(4,128)} %copy-done.24) | copy-start | bytes 18436
  226.7 9.9 %copy-start.27 = (f32[3,512,1]{1,0,2:T(4,128)S(1)}, f32[3,512,1]{1,0,2:T(4,128)}, u32[]{:S(2)}) copy-start(f32[3,512,1]{1,0,2:T(4,128)} %copy-done.26) | copy-start | bytes 18436
  (13 other events, 27.7 us)
Sparse Core Ops, SparseCore 0:
  9.8 24.1 all-gather.1
  184.8 15.9 reduce-scatter.4
  203.9 383.8 reduce-scatter.6
